TPU v7x, 256 devices: a whole 4x4x8 slice. The times are simulated.
256 devices in a mesh: hyp: 32 (over y, x, core), head: 8 (over z).
Axes of the slice: x: 4, y: 4, z: 8, core: 2. Of those that a mesh axis runs over, the one named last changes fastest.
Arguments:
- step_embeds: bfloat16 [3, 512, 4096], P(None, 'hyp'), may hold values from -6 to 6
- lang_table: bfloat16 [8, 4096], replicated, may hold values from -3 to 3
- lang_ids: int32 [32, 4], replicated, may hold values from 0 to 7
- self_gain: float32 [4096], replicated, may hold values from 0.1 to 1.9
- self_wq: bfloat16 [4096, 2048], P(None, 'head'), may hold values from -0.09375 to 0.09375
- self_wk: bfloat16 [4096, 2048], P(None, 'head'), may hold values from -0.09375 to 0.09375
- self_wv: bfloat16 [4096, 2048], P(None, 'head'), may hold values from -0.09375 to 0.09375
- self_wo: bfloat16 [2048, 4096], P('head'), may hold values from -0.125 to 0.125
- cross_gain: float32 [4096], replicated, may hold values from 0.1 to 1.9
- cross_wq: bfloat16 [4096, 2048], P(None, 'head'), may hold values from -0.09375 to 0.09375
- cross_wkv: bfloat16 [4096, 4096], P('hyp', 'head'), may hold values from -0.09375 to 0.09375
- encoder_rows: bfloat16 [24576, 4096], P('hyp', 'head'), may hold values from -200 to 200
- doc_lengths: int32 [32], P('hyp'), may hold values from 192 to 768, as said below
- past_keys: bfloat16 [512, 32, 2048], P('hyp', None, 'head'), may hold values from -200 to 200
- past_values: bfloat16 [512, 32, 2048], P('hyp', None, 'head'), may hold values from -6 to 6
- parents: int32 [3, 512], replicated, may hold values from 0 to 3
Outputs:
- cross_context: bfloat16 [3, 512, 2048], P(None, 'hyp', 'head')
- final_keys: bfloat16 [512, 35, 2048], P('hyp', None, 'head')
- final_values: bfloat16 [512, 35, 2048], P('hyp', None, 'head')
Inputs may be any that keep to these rules, and one draw needn't show every extreme that they name: `doc_lengths`: some document has exactly 768 live rows. `parents`: A parent is a beam of the same document and target.
All inputs are finite; a program needn't handle non-finite values.
Results may differ from a plain program's by a relative error of at most 0.03.
Values may be sent and summed in bfloat16 or wider, within the bound.
No kernel may reach another device: no remote copies, remote signals or barrier semaphores. Data moves between devices by JAX's collectives and lax.ppermute only.
A program may use at most 128 MiB of HBM per device.

v0:
```python
import jax
import jax.numpy as jnp
from jax import lax
from jax.sharding import PartitionSpec as P

HEAD = 256
BEAMS = 4
TARGETS = 4
STEPS = 3
EPSILON = 1e-06


def shifted(block, axis, distance):
    devices = range(lax.axis_size(axis))
    route = [((i - distance) % len(devices), i) for i in devices]
    return lax.ppermute(block, axis, route)


def rms_scaled(values_in, gain):
    mean_square = jnp.mean(values_in * values_in, axis=-1, keepdims=True)
    return values_in * lax.rsqrt(mean_square + EPSILON) * gain


def pick_rows(candidates, selector, row_axis):
    shape_list = [1] * candidates[0].ndim
    shape_list[row_axis] = selector.shape[0]
    chosen = candidates[0]
    for position in range(1, len(candidates)):
        chosen = jnp.where((selector == position).reshape(shape_list), candidates[position], chosen)
    return chosen


def partial_attend(queries, cache_stack, scaling):
    row_count = cache_stack.shape[1]
    cached = cache_stack.shape[2]
    heads_here = cache_stack.shape[3] // HEAD
    key_part = cache_stack[0].reshape(row_count, cached, heads_here, HEAD)
    value_part = cache_stack[1].reshape(row_count, cached, heads_here, HEAD).astype(jnp.float32)
    scores = (
        jnp.einsum(
            "rhd,rphd->rhp",
            queries.reshape(row_count, heads_here, HEAD),
            key_part,
            preferred_element_type=jnp.float32,
        )
        * scaling
    )
    highest = jnp.max(scores, axis=2)
    raw_weights = jnp.exp(scores - highest[:, :, None])
    totals = jnp.sum(raw_weights, axis=2)
    summed = jnp.einsum("rhp,rphd->rhd", raw_weights, value_part)
    return (highest, totals, summed)


def cross_attend(queries, cross_keys, cross_values, doc_length, scaling):
    query_rows = queries.shape[0]
    heads_here = cross_keys.shape[1]
    scores = (
        jnp.einsum(
            "qhd,jhd->hqj",
            queries.reshape(query_rows, heads_here, HEAD),
            cross_keys,
            preferred_element_type=jnp.float32,
        )
        * scaling
    )
    live_mask = lax.broadcasted_iota(jnp.int32, (1, 1, cross_keys.shape[0]), 2) < doc_length
    scores = jnp.where(live_mask, scores, -jnp.inf)
    highest = jnp.max(scores, axis=2, keepdims=True)
    raw_weights = jnp.exp(scores - highest)
    totals = jnp.sum(raw_weights, axis=2, keepdims=True)
    weights = (raw_weights / totals).astype(jnp.bfloat16)
    output = jnp.einsum("hqj,jhd->qhd", weights, cross_values, preferred_element_type=jnp.float32)
    return output.reshape(query_rows, heads_here * HEAD).astype(jnp.bfloat16)


def shards(
    step_embeds,
    lang_table,
    lang_ids,
    self_gain,
    self_wq,
    self_wk,
    self_wv,
    self_wo,
    cross_gain,
    cross_wq,
    cross_wkv,
    encoder_rows,
    doc_lengths,
    past_keys,
    past_values,
    parents,
):
    hyp_count = lax.axis_size("hyp")
    group_size = hyp_count // BEAMS
    my_index = lax.axis_index("hyp")
    my_beam = my_index // group_size
    my_slot = my_index % group_size
    row_count = step_embeds.shape[1]
    head_width = self_wq.shape[1]
    heads_here = head_width // HEAD
    doc_count = lang_ids.shape[0]
    scaling = HEAD ** (-0.5)
    my_langs = lax.dynamic_slice_in_dim(lang_ids, my_slot * BEAMS, BEAMS, 0).reshape(row_count)
    one_hot = (
        my_langs[:, None] == lax.broadcasted_iota(jnp.int32, (1, lang_table.shape[0]), 1)
    ).astype(jnp.bfloat16)
    lang_rows = jnp.dot(one_hot, lang_table, preferred_element_type=jnp.float32)
    full_weights = lax.all_gather(cross_wkv, "hyp", axis=0, tiled=True)
    cross_kv = jnp.dot(
        lax.all_gather(encoder_rows, "head", axis=1, tiled=True),
        full_weights,
        preferred_element_type=jnp.float32,
    ).astype(jnp.bfloat16)
    cross_kv = cross_kv.reshape(encoder_rows.shape[0], heads_here, 2, HEAD)
    cross_keys = cross_kv[:, :, 0, :]
    cross_values = cross_kv[:, :, 1, :]
    doc_length = doc_lengths[0]
    parent_view = parents.reshape(parents.shape[0], BEAMS, -1)
    my_parents = lax.dynamic_slice_in_dim(parent_view, my_slot * row_count, row_count, 2)
    own_parents = lax.dynamic_index_in_dim(my_parents, my_beam, 1, keepdims=False)
    contexts = []
    cache_stack = jnp.stack([past_keys, past_values])
    for step_idx in range(STEPS):
        offsets = (my_beam - own_parents[step_idx]) % BEAMS
        moved_list = [cache_stack]
        for peer_hop in range(1, BEAMS):
            moved_list.append(shifted(cache_stack, "hyp", peer_hop * group_size))
        cache_stack = pick_rows(moved_list, offsets, 1)
        start_hidden_in = step_embeds[step_idx].astype(jnp.float32) + lang_rows
        normed = rms_scaled(start_hidden_in, self_gain).astype(jnp.bfloat16)
        new_query = jnp.dot(normed, self_wq, preferred_element_type=jnp.float32).astype(
            jnp.bfloat16
        )
        new_key = jnp.dot(normed, self_wk, preferred_element_type=jnp.float32).astype(jnp.bfloat16)
        new_value = jnp.dot(normed, self_wv, preferred_element_type=jnp.float32).astype(
            jnp.bfloat16
        )
        fresh_rows = jnp.stack([new_key, new_value])[:, :, None, :]
        hidden_in, new_query, fresh_rows = (start_hidden_in, new_query, fresh_rows)
        cache_stack = jnp.concatenate([cache_stack, fresh_rows], axis=2)
        attn_parts = partial_attend(new_query, cache_stack, scaling)
        rows_here = hidden_in.shape[0]
        self_context = (
            (attn_parts[2] / attn_parts[1][:, :, None])
            .reshape(rows_here, head_width)
            .astype(jnp.bfloat16)
        )
        partial_out = jnp.dot(self_context, self_wo, preferred_element_type=jnp.float32)
        residual = hidden_in + lax.psum(partial_out.astype(jnp.bfloat16), "head").astype(
            jnp.float32
        )
        normed_cross = rms_scaled(residual, cross_gain).astype(jnp.bfloat16)
        cross_query = jnp.dot(normed_cross, cross_wq, preferred_element_type=jnp.float32).astype(
            jnp.bfloat16
        )
        every_query = lax.all_gather(cross_query, "hyp", axis=0, tiled=True)
        arranged = every_query.reshape(BEAMS, doc_count, TARGETS, head_width)
        doc_queries = lax.dynamic_index_in_dim(arranged, my_index, 1, keepdims=False)
        answer = cross_attend(
            doc_queries.reshape(BEAMS * TARGETS, head_width),
            cross_keys,
            cross_values,
            doc_length,
            scaling,
        )
        every_answer = lax.all_gather(answer, "hyp", axis=0, tiled=True)
        by_owner = every_answer.reshape(doc_count, BEAMS, TARGETS, head_width)
        my_block = lax.dynamic_slice_in_dim(by_owner, my_slot * BEAMS, BEAMS, 0)
        contexts.append(
            lax.dynamic_index_in_dim(my_block, my_beam, 1, keepdims=False).reshape(
                row_count, head_width
            )
        )
    return (jnp.stack(contexts), cache_stack[0], cache_stack[1])


def solution(mesh):
    return jax.shard_map(
        shards,
        mesh=mesh,
        in_specs=(
            P(None, "hyp", None),
            P(),
            P(),
            P(),
            P(None, "head"),
            P(None, "head"),
            P(None, "head"),
            P("head", None),
            P(),
            P(None, "head"),
            P("hyp", "head"),
            P("hyp", "head"),
            P("hyp"),
            P("hyp", None, "head"),
            P("hyp", None, "head"),
            P(),
        ),
        out_specs=(P(None, "hyp", "head"), P("hyp", None, "head"), P("hyp", None, "head")),
        check_vma=False,
    )
```

profile of v0, /device:TPU:1, one launch (start us, length us, event | category | flops | bytes accessed | tf_op | source)
XLA Modules:
  0.0 360.1 jit_solution(13073119696567710992)
XLA Ops:
  8.1 1.5 copy_bitcast_fusion
  10.4 3.6 collective-permute-start
  15.9 2.7 fusion.11
  22.4 2.8 fusion.9
  27.1 8.9 %collective-permute-done = bf16[2,16,32,256]{3,1,2,0:T(8,128)(2,1)} collective-permute-done((bf16[2,16,32,256]{3,1,2,0:T(8,128)(2,1)}, bf16[2,16,32,256]{3,1,2,0:T(8,128)(2,1)}, u32[]{:S(2)}, u32[]{:S(2)}) %collective-permute-start) | collective-permute-done | bytes 524320 | tf_op jit(solution)/shard_map/ppermute | solution.py:16
  36.0 4.9 %collective-permute-done.2 = bf16[2,16,32,256]{3,1,2,0:T(8,128)(2,1)} collective-permute-done((bf16[2,16,32,256]{3,1,2,0:T(8,128)(2,1)}, bf16[2,16,32,256]{3,1,2,0:T(8,128)(2,1)}, u32[]{:S(2)}, u32[]{:S(2)}) %collective-permute-start.2) | collective-permute-done | bytes 524320 | tf_op jit(solution)/shard_map/ppermute | solution.py:16
  40.9 1.5 select_select_fusion.2
  45.9 10.0 %collective-permute-done.3 = bf16[2,16,33,256]{3,1,2,0:T(8,128)(2,1)S(1)} collective-permute-done((bf16[2,16,33,256]{3,1,2,0:T(8,128)(2,1)S(1)}, bf16[2,16,33,256]{3,1,2,0:T(8,128)(2,1)S(1)}, u32[]{:S(2)}, u32[]{:S(2)}) %collective-permute-start.3) | collective-permute-done | bytes 540704 | tf_op jit(solution)/shard_map/ppermute | solution.py:16
  55.9 1.1 collective-permute-done.4
  57.0 12.9 %collective-permute-done.5 = bf16[2,16,33,256]{3,1,2,0:T(8,128)(2,1)S(1)} collective-permute-done((bf16[2,16,33,256]{3,1,2,0:T(8,128)(2,1)S(1)}, bf16[2,16,33,256]{3,1,2,0:T(8,128)(2,1)S(1)}, u32[]{:S(2)}, u32[]{:S(2)}) %collective-permute-start.5) | collective-permute-done | bytes 540704 | tf_op jit(solution)/shard_map/ppermute | solution.py:16
  73.6 10.3 %collective-permute-done.6 = bf16[2,16,34,256]{3,1,2,0:T(8,128)(2,1)S(1)} collective-permute-done((bf16[2,16,34,256]{3,1,2,0:T(8,128)(2,1)S(1)}, bf16[2,16,34,256]{3,1,2,0:T(8,128)(2,1)S(1)}, u32[]{:S(2)}, u32[]{:S(2)}) %collective-permute-start.6) | collective-permute-done | bytes 557088 | tf_op jit(solution)/shard_map/ppermute | solution.py:16
  84.6 13.7 %collective-permute-done.8 = bf16[2,16,34,256]{3,1,2,0:T(8,128)(2,1)S(1)} collective-permute-done((bf16[2,16,34,256]{3,1,2,0:T(8,128)(2,1)S(1)}, bf16[2,16,34,256]{3,1,2,0:T(8,128)(2,1)S(1)}, u32[]{:S(2)}, u32[]{:S(2)}) %collective-permute-start.8) | collective-permute-done | bytes 557088 | tf_op jit(solution)/shard_map/ppermute | solution.py:16
  103.0 72.8 %all-reduce.3.cloned.1.call-done = (bf16[16,4096]{1,0:T(8,128)(2,1)}, bf16[16,4096]{1,0:T(8,128)(2,1)}, bf16[16,4096]{1,0:T(8,128)(2,1)}) async-done(((bf16[16,4096]{1,0:T(8,128)(2,1)}, bf16[16,4096]{1,0:T(8,128)(2,1)}, bf16[16,4096]{1,0:T(8,128)(2,1)}), (bf16[16,4096]{1,0:T(8,128)(2,1)}, bf16[16,4096]{1,0:T(8,128)(2,1)}, bf16[16,4096]{1,0:T(8,128)(2,1)})) %all-reduce.3.cloned.1.call-update) | async-done | bytes 393232 | tf_op jit(solution)/shard_map/psum | solution.py:151
  175.8 1.8 multiply_reduce_fusion.4
  177.6 2.1 convolution_convert_fusion.4
  179.7 37.9 %all_gather.30 = bf16[512,256]{1,0:T(8,128)(2,1)S(1)} all-gather(bf16[16,256]{1,0:T(8,128)(2,1)S(1)} %convolution_convert_fusion.4), channel_id=1, replica_groups=mesh['hyp'=32,'head'=8] {'hyp'}, dimensions={0}, use_global_device_ids=true | all-gather | bytes 270336 | tf_op jit(solution)/shard_map/all_gather | solution.py:158
  218.9 2.0 convolution_convert_fusion.8
  220.9 24.2 %all_gather.28 = bf16[512,256]{1,0:T(8,128)(2,1)S(1)} all-gather(bf16[16,256]{1,0:T(8,128)(2,1)S(1)} %convolution_convert_fusion.8), channel_id=1, replica_groups=mesh['hyp'=32,'head'=8] {'hyp'}, dimensions={0}, use_global_device_ids=true | all-gather | bytes 270336 | tf_op jit(solution)/shard_map/all_gather | solution.py:158
  245.8 2.0 convolution_convert_fusion.12
  247.8 22.6 %all_gather.26 = bf16[512,256]{1,0:T(8,128)(2,1)S(1)} all-gather(bf16[16,256]{1,0:T(8,128)(2,1)S(1)} %convolution_convert_fusion.12), channel_id=1, replica_groups=mesh['hyp'=32,'head'=8] {'hyp'}, dimensions={0}, use_global_device_ids=true | all-gather | bytes 270336 | tf_op jit(solution)/shard_map/all_gather | solution.py:158
  270.7 7.5 %convolution_convert_fusion.3 = bf16[768,512]{0,1:T(8,128)(2,1)S(1)} fusion(bf16[768,4096]{1,0:T(8,128)(2,1)} %all-gather.6.cloned.1.call-done, bf16[4096,512]{1,0:T(8,128)(2,1)} %all-gather.8.cloned.1.call-done), kind=kOutput, calls=%fused_computation.3 | convolution fusion | flops 3221618688 | bytes 11272192 | tf_op jit(solution)/shard_map/dot_general | solution.py:111
  278.9 24.5 %all-gather.2 = bf16[512,1,256]{2,0,1:T(8,128)(2,1)S(1)} all-gather(bf16[16,1,256]{2,0,1:T(8,128)(2,1)S(1)} %fusion.14), channel_id=4, replica_groups=mesh['hyp'=32,'head'=8] {'hyp'}, dimensions={0}, use_global_device_ids=true | all-gather | bytes 270336 | tf_op jit(solution)/shard_map/all_gather | solution.py:168
  304.2 22.7 %all-gather.1 = bf16[512,1,256]{2,0,1:T(8,128)(2,1)S(1)} all-gather(bf16[16,1,256]{2,0,1:T(8,128)(2,1)S(1)} %fusion.13), channel_id=3, replica_groups=mesh['hyp'=32,'head'=8] {'hyp'}, dimensions={0}, use_global_device_ids=true | all-gather | bytes 270336 | tf_op jit(solution)/shard_map/all_gather | solution.py:168
  327.7 24.3 %all-gather = bf16[512,1,256]{2,0,1:T(8,128)(2,1)S(1)} all-gather(bf16[16,1,256]{2,0,1:T(8,128)(2,1)S(1)} %fusion.12), channel_id=2, replica_groups=mesh['hyp'=32,'head'=8] {'hyp'}, dimensions={0}, use_global_device_ids=true | all-gather | bytes 270336 | tf_op jit(solution)/shard_map/all_gather | solution.py:168
  (145 shorter events, 25.2 us)
Async XLA Ops:
  8.0 36.8 %copy-start = (bf16[256,4096]{1,0:T(8,128)(2,1)S(1)}, bf16[256,4096]{1,0:T(8,128)(2,1)}, u32[]{:S(2)}) copy-start(bf16[256,4096]{1,0:T(8,128)(2,1)} %param.23) | copy-start | bytes 6291460
  8.0 7.2 %copy-start.4 = (bf16[3,16,4096]{2,1,0:T(8,128)(2,1)S(1)}, bf16[3,16,4096]{2,1,0:T(8,128)(2,1)}, u32[]{:S(2)}) copy-start(bf16[3,16,4096]{2,1,0:T(8,128)(2,1)} %param.16) | copy-start | bytes 1179652
  8.0 7.2 %copy-start.24 = (bf16[8,4096]{1,0:T(8,128)(2,1)S(1)}, bf16[8,4096]{1,0:T(8,128)(2,1)}, u32[]{:S(2)}) copy-start(bf16[8,4096]{1,0:T(8,128)(2,1)} %param.17) | copy-start | bytes 196612
  8.0 7.7 %copy-start.17 = (f32[4096]{0:T(1024)S(1)}, f32[4096]{0:T(1024)}, u32[]{:S(2)}) copy-start(f32[4096]{0:T(1024)} %param.19) | copy-start | bytes 49156
  8.1 167.7 %all-reduce.3.cloned.1.call-start = ((), (), s32[]{:S(2)}) async-start(), calls=%async_computation.2 | async-start | bytes 786432 | tf_op jit(solution)/shard_map/psum | solution.py:151
  10.4 25.6 %collective-permute-start = (bf16[2,16,32,256]{3,1,2,0:T(8,128)(2,1)}, bf16[2,16,32,256]{3,1,2,0:T(8,128)(2,1)}, u32[]{:S(2)}, u32[]{:S(2)}) collective-permute-start(bf16[2,16,32,256]{3,1,2,0:T(8,128)(2,1)} %pad_maximum_fusion.2), channel_id=1, source_target_pairs={{64,0},{72,8},{80,16},{88,24},{96,32},{104,40},{112,48},{120,56},{... | collective-permute-start | bytes 1572872 | tf_op jit(solution)/shard_map/ppermute | solution.py:16
  14.0 22.0 %collective-permute-start.1 = (bf16[2,16,32,256]{3,1,2,0:T(8,128)(2,1)}, bf16[2,16,32,256]{3,1,2,0:T(8,128)(2,1)}, u32[]{:S(2)}, u32[]{:S(2)}) collective-permute-start(bf16[2,16,32,256]{3,1,2,0:T(8,128)(2,1)} %pad_maximum_fusion.2), channel_id=1, source_target_pairs={{128,0},{136,8},{144,16},{152,24},{160,32},{168,40},{176,48},{184,... | collective-permute-start | bytes 1572872 | tf_op jit(solution)/shard_map/ppermute | solution.py:16
  14.3 26.6 %collective-permute-start.2 = (bf16[2,16,32,256]{3,1,2,0:T(8,128)(2,1)}, bf16[2,16,32,256]{3,1,2,0:T(8,128)(2,1)}, u32[]{:S(2)}, u32[]{:S(2)}) collective-permute-start(bf16[2,16,32,256]{3,1,2,0:T(8,128)(2,1)} %pad_maximum_fusion.2), channel_id=1, source_target_pairs={{192,0},{200,8},{208,16},{216,24},{224,32},{232,40},{240,48},{248,... | collective-permute-start | bytes 1572872 | tf_op jit(solution)/shard_map/ppermute | solution.py:16
  42.5 13.4 %collective-permute-start.3 = (bf16[2,16,33,256]{3,1,2,0:T(8,128)(2,1)S(1)}, bf16[2,16,33,256]{3,1,2,0:T(8,128)(2,1)S(1)}, u32[]{:S(2)}, u32[]{:S(2)}) collective-permute-start(bf16[2,16,33,256]{3,1,2,0:T(8,128)(2,1)S(1)} %pad_maximum_fusion.1), channel_id=1, source_target_pairs={{64,0},{72,8},{80,16},{88,24},{96,32},{104,40},{112,48},{120,56},{... | collective-permute-start | bytes 1622024 | tf_op jit(solution)/shard_map/ppermute | solution.py:16
  42.6 14.5 %collective-permute-start.4 = (bf16[2,16,33,256]{3,1,2,0:T(8,128)(2,1)S(1)}, bf16[2,16,33,256]{3,1,2,0:T(8,128)(2,1)S(1)}, u32[]{:S(2)}, u32[]{:S(2)}) collective-permute-start(bf16[2,16,33,256]{3,1,2,0:T(8,128)(2,1)S(1)} %pad_maximum_fusion.1), channel_id=1, source_target_pairs={{128,0},{136,8},{144,16},{152,24},{160,32},{168,40},{176,48},{184,... | collective-permute-start | bytes 1622024 | tf_op jit(solution)/shard_map/ppermute | solution.py:16
  43.0 26.9 %collective-permute-start.5 = (bf16[2,16,33,256]{3,1,2,0:T(8,128)(2,1)S(1)}, bf16[2,16,33,256]{3,1,2,0:T(8,128)(2,1)S(1)}, u32[]{:S(2)}, u32[]{:S(2)}) collective-permute-start(bf16[2,16,33,256]{3,1,2,0:T(8,128)(2,1)S(1)} %pad_maximum_fusion.1), channel_id=1, source_target_pairs={{192,0},{200,8},{208,16},{216,24},{224,32},{232,40},{240,48},{248,... | collective-permute-start | bytes 1622024 | tf_op jit(solution)/shard_map/ppermute | solution.py:16
  70.2 13.8 %collective-permute-start.6 = (bf16[2,16,34,256]{3,1,2,0:T(8,128)(2,1)S(1)}, bf16[2,16,34,256]{3,1,2,0:T(8,128)(2,1)S(1)}, u32[]{:S(2)}, u32[]{:S(2)}) collective-permute-start(bf16[2,16,34,256]{3,1,2,0:T(8,128)(2,1)S(1)} %pad_maximum_fusion), channel_id=1, source_target_pairs={{64,0},{72,8},{80,16},{88,24},{96,32},{104,40},{112,48},{120,56},{... | collective-permute-start | bytes 1671176 | tf_op jit(solution)/shard_map/ppermute | solution.py:16
  70.2 14.4 %collective-permute-start.7 = (bf16[2,16,34,256]{3,1,2,0:T(8,128)(2,1)S(1)}, bf16[2,16,34,256]{3,1,2,0:T(8,128)(2,1)S(1)}, u32[]{:S(2)}, u32[]{:S(2)}) collective-permute-start(bf16[2,16,34,256]{3,1,2,0:T(8,128)(2,1)S(1)} %pad_maximum_fusion), channel_id=1, source_target_pairs={{128,0},{136,8},{144,16},{152,24},{160,32},{168,40},{176,48},{184,... | collective-permute-start | bytes 1671176 | tf_op jit(solution)/shard_map/ppermute | solution.py:16
  70.7 27.6 %collective-permute-start.8 = (bf16[2,16,34,256]{3,1,2,0:T(8,128)(2,1)S(1)}, bf16[2,16,34,256]{3,1,2,0:T(8,128)(2,1)S(1)}, u32[]{:S(2)}, u32[]{:S(2)}) collective-permute-start(bf16[2,16,34,256]{3,1,2,0:T(8,128)(2,1)S(1)} %pad_maximum_fusion), channel_id=1, source_target_pairs={{192,0},{200,8},{208,16},{216,24},{224,32},{232,40},{240,48},{248,... | collective-permute-start | bytes 1671176 | tf_op jit(solution)/shard_map/ppermute | solution.py:16
  73.6 25.0 %copy-start.19 = (bf16[16,256,1]{1,0,2:T(8,128)(2,1)S(1)}, bf16[16,256,1]{1,0,2:T(8,128)(2,1)}, u32[]{:S(2)}) copy-start(bf16[16,256,1]{1,0,2:T(8,128)(2,1)} %fusion.9) | copy-start | bytes 24580
  99.5 78.1 %copy-start.10 = (f32[4096]{0:T(1024)S(1)}, f32[4096]{0:T(1024)}, u32[]{:S(2)}) copy-start(f32[4096]{0:T(1024)} %param.24) | copy-start | bytes 49156
  100.6 170.0 %all-gather.8.cloned.1.call-start = ((), (), s32[]{:S(2)}) async-start(), calls=%async_computation.1 | async-start | bytes 4325376 | tf_op jit(solution)/shard_map/all_gather | solution.py:110
  101.2 169.5 %all-gather.6.cloned.1.call-start = ((), (), s32[]{:S(2)}) async-start(), calls=%async_computation | async-start | bytes 7077888 | tf_op jit(solution)/shard_map/all_gather | solution.py:112
  175.8 43.1 %copy-start.8 = (bf16[16,4096]{1,0:T(8,128)(2,1)S(1)}, bf16[16,4096]{1,0:T(8,128)(2,1)}, u32[]{:S(2)}) copy-start(bf16[16,4096]{1,0:T(8,128)(2,1)} %get-tuple-element.11) | copy-start | bytes 393220
  179.7 66.1 %copy-start.7 = (bf16[16,4096]{1,0:T(8,128)(2,1)S(1)}, bf16[16,4096]{1,0:T(8,128)(2,1)}, u32[]{:S(2)}) copy-start(bf16[16,4096]{1,0:T(8,128)(2,1)} %get-tuple-element.10) | copy-start | bytes 393220
  217.7 28.1 %copy-start.23 = (f32[16]{0:T(128)S(1)}, f32[16]{0:T(128)}, u32[]{:S(2)}) copy-start(f32[16]{0:T(128)} %get-tuple-element.3) | copy-start | bytes 196
  270.6 7.6 %copy-start.12 = (bf16[16,256]{1,0:T(8,128)(2,1)S(1)}, bf16[16,256]{1,0:T(8,128)(2,1)}, u32[]{:S(2)}) copy-start(bf16[16,256]{1,0:T(8,128)(2,1)} %reshape.403) | copy-start | bytes 24580
  270.6 7.6 %copy-start.18 = (pred[768]{0:T(1024)(128)(4,1)S(1)}, pred[768]{0:T(1024)(128)(4,1)}, u32[]{:S(2)}) copy-start(pred[768]{0:T(1024)(128)(4,1)} %iota_compare_fusion.2) | copy-start | bytes 2308
  270.6 32.9 %copy-start.11 = (bf16[16,256]{1,0:T(8,128)(2,1)S(1)}, bf16[16,256]{1,0:T(8,128)(2,1)}, u32[]{:S(2)}) copy-start(bf16[16,256]{1,0:T(8,128)(2,1)} %reshape.398) | copy-start | bytes 24580
  (13 other events, 29.6 us)
Sparse Core Ops, SparseCore 0:
  100.7 74.9 all-reduce.2
Sparse Core Ops, SparseCore 1:
  103.7 52.1 all-gather.7
  157.5 73.3 all-gather.5
where the time goes:
time: 360 us
  blocking collectives  156 us (43%)
  waiting for transfers between devices  136 us (38%)
  matrix products  30.7 us (9%)
  between operations  16.7 us (5%)
  other arithmetic  8.37 us (2%)
  starting transfers between devices  7.79 us (2%)
  local copies, waits for them, and re-layouts  4.05 us (1%)
    all_gather x3, blocking collectives, shards(): every_query = lax.all_gather(cross_query, 'hyp', axis=0, tiled=True)  84.7 us
    psum x1, waiting for transfers between devices, shards(): lax.psum(partial_out.astype(jnp.bfloat16), 'head').astype(jnp.float32)  72.8 us
    all_gather x3, blocking collectives, shards(): every_answer = lax.all_gather(answer, 'hyp', axis=0, tiled=True)  71.4 us
    ppermute x9, waiting for transfers between devices, shifted(): return lax.ppermute(block, axis, route)  62.5 us
    ppermute x9, starting transfers between devices, shifted(): return lax.ppermute(block, axis, route)  7.67 us
    dot_general x1, matrix products, shards(): jnp.dot(lax.all_gather(encoder_rows, 'head', axis=1, tiled=True), full_we...  7.47 us
  transfers between devices with their start and end apart: 12, of which 9 were waited for; matrix products, arithmetic and copies ran while one was open for 7% of the time, Pallas kernels for 0%

commit v1 on v0

--- a/solution.py
+++ b/solution.py
@@ -165,7 +165,9 @@
             doc_length,
             scaling,
         )
-        every_answer = lax.all_gather(answer, "hyp", axis=0, tiled=True)
+        every_answer = jnp.concatenate(
+            lax.all_to_all(jnp.stack([answer] * lax.axis_size("hyp")), "hyp", 0, 0), axis=0
+        )
         by_owner = every_answer.reshape(doc_count, BEAMS, TARGETS, head_width)
         my_block = lax.dynamic_slice_in_dim(by_owner, my_slot * BEAMS, BEAMS, 0)
         contexts.append(

time: 360 us -> 329 us (0.914)
  blocking collectives: 156 us -> 84.7 us
  waiting for transfers between devices: 136 us -> 161 us
  starting transfers between devices: 7.79 us -> 20.3 us
    all_gather x3 -> x0, blocking collectives: 71.4 us -> none  [shards(): every_answer = lax.all_gather(answer, 'hyp', axis=0, tiled=True)]
    all_to_all x0 -> x3, waiting for transfers between devices: none -> 24.9 us  [shards(): lax.all_to_all(jnp.stack([answer] * lax.axis_size('hyp')), 'hyp', 0, 0)]
    all_to_all x0 -> x3, starting transfers between devices: none -> 12.5 us  [shards(): lax.all_to_all(jnp.stack([answer] * lax.axis_size('hyp')), 'hyp', 0, 0)]
  transfers between devices with their start and end apart: 12 -> 15, of which waited for: 9 -> 12; matrix products, arithmetic and copies ran while one was open for 7% -> 8% of each run, Pallas kernels for 0% -> 0%
where the time goes in v1:
time: 329 us
  waiting for transfers between devices  161 us (49%)
  blocking collectives  84.7 us (26%)
  matrix products  30.8 us (9%)
  starting transfers between devices  20.3 us (6%)
  between operations  16.7 us (5%)
  other arithmetic  8.45 us (3%)
  local copies, waits for them, and re-layouts  6.38 us (2%)
    all_gather x3, blocking collectives, shards(): every_query = lax.all_gather(cross_query, 'hyp', axis=0, tiled=True)  84.7 us
    psum x1, waiting for transfers between devices, shards(): lax.psum(partial_out.astype(jnp.bfloat16), 'head').astype(jnp.float32)  72.7 us
    ppermute x9, waiting for transfers between devices, shifted(): return lax.ppermute(block, axis, route)  62.5 us
    all_to_all x3, waiting for transfers between devices, shards(): lax.all_to_all(jnp.stack([answer] * lax.axis_size('hyp')), 'hyp', 0, 0)  24.9 us
    all_to_all x3, starting transfers between devices, shards(): lax.all_to_all(jnp.stack([answer] * lax.axis_size('hyp')), 'hyp', 0, 0)  12.5 us
    ppermute x9, starting transfers between devices, shifted(): return lax.ppermute(block, axis, route)  7.67 us
    dot_general x1, matrix products, shards(): jnp.dot(lax.all_gather(encoder_rows, 'head', axis=1, tiled=True), full_we...  7.47 us
  transfers between devices with their start and end apart: 15, of which 12 were waited for; matrix products, arithmetic and copies ran while one was open for 8% of the time, Pallas kernels for 0%

profile of v1, /device:TPU:1, one launch (start us, length us, event | category | flops | bytes accessed | tf_op | source)
XLA Modules:
  0.0 328.6 jit_solution(2811271808512658126)
XLA Ops:
  10.4 3.6 %collective-permute-start = (bf16[2,16,32,256]{3,1,2,0:T(8,128)(2,1)}, bf16[2,16,32,256]{3,1,2,0:T(8,128)(2,1)}, u32[]{:S(2)}, u32[]{:S(2)}) collective-permute-start(bf16[2,16,32,256]{3,1,2,0:T(8,128)(2,1)} %pad_maximum_fusion.2), channel_id=1, source_target_pairs={{64,0},{72,8},{80,16},{88,24},{96,32},{104,40},{112,48},{120,56},{... | collective-permute-start | bytes 1572872 | tf_op jit(solution)/shard_map/ppermute | solution.py:16
  15.9 2.7 fusion.11
  22.4 2.8 fusion.9
  27.1 8.9 %collective-permute-done = bf16[2,16,32,256]{3,1,2,0:T(8,128)(2,1)} collective-permute-done((bf16[2,16,32,256]{3,1,2,0:T(8,128)(2,1)}, bf16[2,16,32,256]{3,1,2,0:T(8,128)(2,1)}, u32[]{:S(2)}, u32[]{:S(2)}) %collective-permute-start) | collective-permute-done | bytes 524320 | tf_op jit(solution)/shard_map/ppermute | solution.py:16
  36.0 4.9 %collective-permute-done.2 = bf16[2,16,32,256]{3,1,2,0:T(8,128)(2,1)} collective-permute-done((bf16[2,16,32,256]{3,1,2,0:T(8,128)(2,1)}, bf16[2,16,32,256]{3,1,2,0:T(8,128)(2,1)}, u32[]{:S(2)}, u32[]{:S(2)}) %collective-permute-start.2) | collective-permute-done | bytes 524320 | tf_op jit(solution)/shard_map/ppermute | solution.py:16
  45.9 10.0 %collective-permute-done.3 = bf16[2,16,33,256]{3,1,2,0:T(8,128)(2,1)S(1)} collective-permute-done((bf16[2,16,33,256]{3,1,2,0:T(8,128)(2,1)S(1)}, bf16[2,16,33,256]{3,1,2,0:T(8,128)(2,1)S(1)}, u32[]{:S(2)}, u32[]{:S(2)}) %collective-permute-start.3) | collective-permute-done | bytes 540704 | tf_op jit(solution)/shard_map/ppermute | solution.py:16
  57.0 12.9 %collective-permute-done.5 = bf16[2,16,33,256]{3,1,2,0:T(8,128)(2,1)S(1)} collective-permute-done((bf16[2,16,33,256]{3,1,2,0:T(8,128)(2,1)S(1)}, bf16[2,16,33,256]{3,1,2,0:T(8,128)(2,1)S(1)}, u32[]{:S(2)}, u32[]{:S(2)}) %collective-permute-start.5) | collective-permute-done | bytes 540704 | tf_op jit(solution)/shard_map/ppermute | solution.py:16
  73.6 10.3 %collective-permute-done.6 = bf16[2,16,34,256]{3,1,2,0:T(8,128)(2,1)S(1)} collective-permute-done((bf16[2,16,34,256]{3,1,2,0:T(8,128)(2,1)S(1)}, bf16[2,16,34,256]{3,1,2,0:T(8,128)(2,1)S(1)}, u32[]{:S(2)}, u32[]{:S(2)}) %collective-permute-start.6) | collective-permute-done | bytes 557088 | tf_op jit(solution)/shard_map/ppermute | solution.py:16
  84.6 13.7 %collective-permute-done.8 = bf16[2,16,34,256]{3,1,2,0:T(8,128)(2,1)S(1)} collective-permute-done((bf16[2,16,34,256]{3,1,2,0:T(8,128)(2,1)S(1)}, bf16[2,16,34,256]{3,1,2,0:T(8,128)(2,1)S(1)}, u32[]{:S(2)}, u32[]{:S(2)}) %collective-permute-start.8) | collective-permute-done | bytes 557088 | tf_op jit(solution)/shard_map/ppermute | solution.py:16
  103.0 72.7 %all-reduce.3.cloned.1.call-done = (bf16[16,4096]{1,0:T(8,128)(2,1)}, bf16[16,4096]{1,0:T(8,128)(2,1)}, bf16[16,4096]{1,0:T(8,128)(2,1)}) async-done(((bf16[16,4096]{1,0:T(8,128)(2,1)}, bf16[16,4096]{1,0:T(8,128)(2,1)}, bf16[16,4096]{1,0:T(8,128)(2,1)}), (bf16[16,4096]{1,0:T(8,128)(2,1)}, bf16[16,4096]{1,0:T(8,128)(2,1)}, bf16[16,4096]{1,0:T(8,128)(2,1)})) %all-reduce.3.cloned.1.call-update) | async-done | bytes 393232 | tf_op jit(solution)/shard_map/psum | solution.py:151
  175.8 1.9 multiply_reduce_fusion.4
  177.7 2.1 convolution_convert_fusion.4
  179.8 37.9 %all_gather.19 = bf16[512,256]{1,0:T(8,128)(2,1)S(1)} all-gather(bf16[16,256]{1,0:T(8,128)(2,1)S(1)} %convolution_convert_fusion.4), channel_id=1, replica_groups=mesh['hyp'=32,'head'=8] {'hyp'}, dimensions={0}, use_global_device_ids=true | all-gather | bytes 270336 | tf_op jit(solution)/shard_map/all_gather | solution.py:158
  219.0 2.0 convolution_convert_fusion.8
  221.0 24.2 %all_gather.18 = bf16[512,256]{1,0:T(8,128)(2,1)S(1)} all-gather(bf16[16,256]{1,0:T(8,128)(2,1)S(1)} %convolution_convert_fusion.8), channel_id=1, replica_groups=mesh['hyp'=32,'head'=8] {'hyp'}, dimensions={0}, use_global_device_ids=true | all-gather | bytes 270336 | tf_op jit(solution)/shard_map/all_gather | solution.py:158
  245.9 2.0 convolution_convert_fusion.12
  247.9 22.6 %all_gather.17 = bf16[512,256]{1,0:T(8,128)(2,1)S(1)} all-gather(bf16[16,256]{1,0:T(8,128)(2,1)S(1)} %convolution_convert_fusion.12), channel_id=1, replica_groups=mesh['hyp'=32,'head'=8] {'hyp'}, dimensions={0}, use_global_device_ids=true | all-gather | bytes 270336 | tf_op jit(solution)/shard_map/all_gather | solution.py:158
  270.7 7.5 %convolution_convert_fusion.3 = bf16[768,512]{0,1:T(8,128)(2,1)S(1)} fusion(bf16[768,4096]{1,0:T(8,128)(2,1)} %all-gather.3.cloned.1.call-done, bf16[4096,512]{1,0:T(8,128)(2,1)} %all-gather.5.cloned.1.call-done), kind=kOutput, calls=%fused_computation.3 | convolution fusion | flops 3221618688 | bytes 11272192 | tf_op jit(solution)/shard_map/dot_general | solution.py:111
  279.7 5.0 %all-to-all-start.2 = ((bf16[32,16,256]{2,1,0:T(8,128)(2,1)}), bf16[32,16,256]{2,1,0:T(8,128)(2,1)S(1)}, u32[]{:S(2)}, u32[]{:S(2)}) async-start(bf16[32,16,256]{2,1,0:T(8,128)(2,1)} %stack.46), calls=%async_computation.2 | async-start | bytes 524288 | tf_op jit(solution)/shard_map/all_to_all | solution.py:169
  285.8 7.8 %all-to-all-done.2 = bf16[32,16,256]{2,1,0:T(8,128)(2,1)S(1)} async-done(((bf16[32,16,256]{2,1,0:T(8,128)(2,1)}), bf16[32,16,256]{2,1,0:T(8,128)(2,1)S(1)}, u32[]{:S(2)}, u32[]{:S(2)}) %all-to-all-start.2) | async-done | bytes 262176 | tf_op jit(solution)/shard_map/all_to_all | solution.py:169
  294.3 3.8 %all-to-all-start.1 = ((bf16[32,16,256]{2,1,0:T(8,128)(2,1)}), bf16[32,16,256]{2,1,0:T(8,128)(2,1)S(1)}, u32[]{:S(2)}, u32[]{:S(2)}) async-start(bf16[32,16,256]{2,1,0:T(8,128)(2,1)} %stack.42), calls=%async_computation.1 | async-start | bytes 524288 | tf_op jit(solution)/shard_map/all_to_all | solution.py:169
  298.5 8.5 %all-to-all-done.1 = bf16[32,16,256]{2,1,0:T(8,128)(2,1)S(1)} async-done(((bf16[32,16,256]{2,1,0:T(8,128)(2,1)}), bf16[32,16,256]{2,1,0:T(8,128)(2,1)S(1)}, u32[]{:S(2)}, u32[]{:S(2)}) %all-to-all-start.1) | async-done | bytes 262176 | tf_op jit(solution)/shard_map/all_to_all | solution.py:169
  307.7 3.8 %all-to-all-start = ((bf16[32,16,256]{2,1,0:T(8,128)(2,1)}), bf16[32,16,256]{2,1,0:T(8,128)(2,1)S(1)}, u32[]{:S(2)}, u32[]{:S(2)}) async-start(bf16[32,16,256]{2,1,0:T(8,128)(2,1)} %stack.38), calls=%async_computation | async-start | bytes 524288 | tf_op jit(solution)/shard_map/all_to_all | solution.py:169
  311.8 8.6 %all-to-all-done = bf16[32,16,256]{2,1,0:T(8,128)(2,1)S(1)} async-done(((bf16[32,16,256]{2,1,0:T(8,128)(2,1)}), bf16[32,16,256]{2,1,0:T(8,128)(2,1)S(1)}, u32[]{:S(2)}, u32[]{:S(2)}) %all-to-all-start) | async-done | bytes 262176 | tf_op jit(solution)/shard_map/all_to_all | solution.py:169
  (154 shorter events, 31.8 us)
Async XLA Ops:
  8.0 36.8 %copy-start = (bf16[256,4096]{1,0:T(8,128)(2,1)S(1)}, bf16[256,4096]{1,0:T(8,128)(2,1)}, u32[]{:S(2)}) copy-start(bf16[256,4096]{1,0:T(8,128)(2,1)} %param.23) | copy-start | bytes 6291460
  8.0 7.7 %copy-start.17 = (f32[4096]{0:T(1024)S(1)}, f32[4096]{0:T(1024)}, u32[]{:S(2)}) copy-start(f32[4096]{0:T(1024)} %param.19) | copy-start | bytes 49156
  8.1 167.7 %all-reduce.3.cloned.1.call-start = ((), (), s32[]{:S(2)}) async-start(), calls=%async_computation.5 | async-start | bytes 786432 | tf_op jit(solution)/shard_map/psum | solution.py:151
  10.4 25.6 %collective-permute-start = (bf16[2,16,32,256]{3,1,2,0:T(8,128)(2,1)}, bf16[2,16,32,256]{3,1,2,0:T(8,128)(2,1)}, u32[]{:S(2)}, u32[]{:S(2)}) collective-permute-start(bf16[2,16,32,256]{3,1,2,0:T(8,128)(2,1)} %pad_maximum_fusion.2), channel_id=1, source_target_pairs={{64,0},{72,8},{80,16},{88,24},{96,32},{104,40},{112,48},{120,56},{... | collective-permute-start | bytes 1572872 | tf_op jit(solution)/shard_map/ppermute | solution.py:16
  14.0 22.0 %collective-permute-start.1 = (bf16[2,16,32,256]{3,1,2,0:T(8,128)(2,1)}, bf16[2,16,32,256]{3,1,2,0:T(8,128)(2,1)}, u32[]{:S(2)}, u32[]{:S(2)}) collective-permute-start(bf16[2,16,32,256]{3,1,2,0:T(8,128)(2,1)} %pad_maximum_fusion.2), channel_id=1, source_target_pairs={{128,0},{136,8},{144,16},{152,24},{160,32},{168,40},{176,48},{184,... | collective-permute-start | bytes 1572872 | tf_op jit(solution)/shard_map/ppermute | solution.py:16
  14.3 26.6 %collective-permute-start.2 = (bf16[2,16,32,256]{3,1,2,0:T(8,128)(2,1)}, bf16[2,16,32,256]{3,1,2,0:T(8,128)(2,1)}, u32[]{:S(2)}, u32[]{:S(2)}) collective-permute-start(bf16[2,16,32,256]{3,1,2,0:T(8,128)(2,1)} %pad_maximum_fusion.2), channel_id=1, source_target_pairs={{192,0},{200,8},{208,16},{216,24},{224,32},{232,40},{240,48},{248,... | collective-permute-start | bytes 1572872 | tf_op jit(solution)/shard_map/ppermute | solution.py:16
  42.5 13.4 %collective-permute-start.3 = (bf16[2,16,33,256]{3,1,2,0:T(8,128)(2,1)S(1)}, bf16[2,16,33,256]{3,1,2,0:T(8,128)(2,1)S(1)}, u32[]{:S(2)}, u32[]{:S(2)}) collective-permute-start(bf16[2,16,33,256]{3,1,2,0:T(8,128)(2,1)S(1)} %pad_maximum_fusion.1), channel_id=1, source_target_pairs={{64,0},{72,8},{80,16},{88,24},{96,32},{104,40},{112,48},{120,56},{... | collective-permute-start | bytes 1622024 | tf_op jit(solution)/shard_map/ppermute | solution.py:16
  42.6 14.5 %collective-permute-start.4 = (bf16[2,16,33,256]{3,1,2,0:T(8,128)(2,1)S(1)}, bf16[2,16,33,256]{3,1,2,0:T(8,128)(2,1)S(1)}, u32[]{:S(2)}, u32[]{:S(2)}) collective-permute-start(bf16[2,16,33,256]{3,1,2,0:T(8,128)(2,1)S(1)} %pad_maximum_fusion.1), channel_id=1, source_target_pairs={{128,0},{136,8},{144,16},{152,24},{160,32},{168,40},{176,48},{184,... | collective-permute-start | bytes 1622024 | tf_op jit(solution)/shard_map/ppermute | solution.py:16
  43.0 26.9 %collective-permute-start.5 = (bf16[2,16,33,256]{3,1,2,0:T(8,128)(2,1)S(1)}, bf16[2,16,33,256]{3,1,2,0:T(8,128)(2,1)S(1)}, u32[]{:S(2)}, u32[]{:S(2)}) collective-permute-start(bf16[2,16,33,256]{3,1,2,0:T(8,128)(2,1)S(1)} %pad_maximum_fusion.1), channel_id=1, source_target_pairs={{192,0},{200,8},{208,16},{216,24},{224,32},{232,40},{240,48},{248,... | collective-permute-start | bytes 1622024 | tf_op jit(solution)/shard_map/ppermute | solution.py:16
  70.2 13.8 %collective-permute-start.6 = (bf16[2,16,34,256]{3,1,2,0:T(8,128)(2,1)S(1)}, bf16[2,16,34,256]{3,1,2,0:T(8,128)(2,1)S(1)}, u32[]{:S(2)}, u32[]{:S(2)}) collective-permute-start(bf16[2,16,34,256]{3,1,2,0:T(8,128)(2,1)S(1)} %pad_maximum_fusion), channel_id=1, source_target_pairs={{64,0},{72,8},{80,16},{88,24},{96,32},{104,40},{112,48},{120,56},{... | collective-permute-start | bytes 1671176 | tf_op jit(solution)/shard_map/ppermute | solution.py:16
  70.3 14.4 %collective-permute-start.7 = (bf16[2,16,34,256]{3,1,2,0:T(8,128)(2,1)S(1)}, bf16[2,16,34,256]{3,1,2,0:T(8,128)(2,1)S(1)}, u32[]{:S(2)}, u32[]{:S(2)}) collective-permute-start(bf16[2,16,34,256]{3,1,2,0:T(8,128)(2,1)S(1)} %pad_maximum_fusion), channel_id=1, source_target_pairs={{128,0},{136,8},{144,16},{152,24},{160,32},{168,40},{176,48},{184,... | collective-permute-start | bytes 1671176 | tf_op jit(solution)/shard_map/ppermute | solution.py:16
  70.7 27.6 %collective-permute-start.8 = (bf16[2,16,34,256]{3,1,2,0:T(8,128)(2,1)S(1)}, bf16[2,16,34,256]{3,1,2,0:T(8,128)(2,1)S(1)}, u32[]{:S(2)}, u32[]{:S(2)}) collective-permute-start(bf16[2,16,34,256]{3,1,2,0:T(8,128)(2,1)S(1)} %pad_maximum_fusion), channel_id=1, source_target_pairs={{192,0},{200,8},{208,16},{216,24},{224,32},{232,40},{240,48},{248,... | collective-permute-start | bytes 1671176 | tf_op jit(solution)/shard_map/ppermute | solution.py:16
  73.6 25.0 %copy-start.19 = (bf16[16,256,1]{1,0,2:T(8,128)(2,1)S(1)}, bf16[16,256,1]{1,0,2:T(8,128)(2,1)}, u32[]{:S(2)}) copy-start(bf16[16,256,1]{1,0,2:T(8,128)(2,1)} %fusion.9) | copy-start | bytes 24580
  99.5 78.1 %copy-start.10 = (f32[4096]{0:T(1024)S(1)}, f32[4096]{0:T(1024)}, u32[]{:S(2)}) copy-start(f32[4096]{0:T(1024)} %param.24) | copy-start | bytes 49156
  100.6 170.1 %all-gather.5.cloned.1.call-start = ((), (), s32[]{:S(2)}) async-start(), calls=%async_computation.4 | async-start | bytes 4325376 | tf_op jit(solution)/shard_map/all_gather | solution.py:110
  101.2 169.5 %all-gather.3.cloned.1.call-start = ((), (), s32[]{:S(2)}) async-start(), calls=%async_computation.3 | async-start | bytes 7077888 | tf_op jit(solution)/shard_map/all_gather | solution.py:112
  175.8 43.2 %copy-start.8 = (bf16[16,4096]{1,0:T(8,128)(2,1)S(1)}, bf16[16,4096]{1,0:T(8,128)(2,1)}, u32[]{:S(2)}) copy-start(bf16[16,4096]{1,0:T(8,128)(2,1)} %get-tuple-element.11) | copy-start | bytes 393220
  179.8 66.1 %copy-start.7 = (bf16[16,4096]{1,0:T(8,128)(2,1)S(1)}, bf16[16,4096]{1,0:T(8,128)(2,1)}, u32[]{:S(2)}) copy-start(bf16[16,4096]{1,0:T(8,128)(2,1)} %get-tuple-element.10) | copy-start | bytes 393220
  217.7 28.1 %copy-start.23 = (f32[16]{0:T(128)S(1)}, f32[16]{0:T(128)}, u32[]{:S(2)}) copy-start(f32[16]{0:T(128)} %get-tuple-element.3) | copy-start | bytes 196
  270.6 7.6 %copy-start.12 = (bf16[16,256]{1,0:T(8,128)(2,1)S(1)}, bf16[16,256]{1,0:T(8,128)(2,1)}, u32[]{:S(2)}) copy-start(bf16[16,256]{1,0:T(8,128)(2,1)} %reshape.401) | copy-start | bytes 24580
  270.7 14.1 %copy-start.11 = (bf16[16,256]{1,0:T(8,128)(2,1)S(1)}, bf16[16,256]{1,0:T(8,128)(2,1)}, u32[]{:S(2)}) copy-start(bf16[16,256]{1,0:T(8,128)(2,1)} %reshape.397) | copy-start | bytes 24580
  279.7 13.9 %all-to-all-start.2 = ((bf16[32,16,256]{2,1,0:T(8,128)(2,1)}), bf16[32,16,256]{2,1,0:T(8,128)(2,1)S(1)}, u32[]{:S(2)}, u32[]{:S(2)}) async-start(bf16[32,16,256]{2,1,0:T(8,128)(2,1)} %stack.46), calls=%async_computation.2 | async-start | bytes 524288 | tf_op jit(solution)/shard_map/all_to_all | solution.py:169
  294.3 12.7 %all-to-all-start.1 = ((bf16[32,16,256]{2,1,0:T(8,128)(2,1)}), bf16[32,16,256]{2,1,0:T(8,128)(2,1)S(1)}, u32[]{:S(2)}, u32[]{:S(2)}) async-start(bf16[32,16,256]{2,1,0:T(8,128)(2,1)} %stack.42), calls=%async_computation.1 | async-start | bytes 524288 | tf_op jit(solution)/shard_map/all_to_all | solution.py:169
  307.7 12.7 %all-to-all-start = ((bf16[32,16,256]{2,1,0:T(8,128)(2,1)}), bf16[32,16,256]{2,1,0:T(8,128)(2,1)S(1)}, u32[]{:S(2)}, u32[]{:S(2)}) async-start(bf16[32,16,256]{2,1,0:T(8,128)(2,1)} %stack.38), calls=%async_computation | async-start | bytes 524288 | tf_op jit(solution)/shard_map/all_to_all | solution.py:169
  (16 other events, 51.6 us)
Sparse Core Ops, SparseCore 0:
  100.7 74.9 all-reduce.2
Sparse Core Ops, SparseCore 1:
  103.7 52.1 all-gather.4
  157.5 73.3 all-gather.2
